TPU v7x, 128 devices: a whole 4x4x4 slice. The times are simulated.
128 devices in a mesh: req: 4 (over z), vocab: 32 (over y, x, core).
Axes of the slice: x: 4, y: 4, z: 4, core: 2. Of those that a mesh axis runs over, the one named last changes fastest.
Arguments:
- hidden: bfloat16 [16, 1536, 2048], P('req', 'vocab'), may hold values from -80 to 80
- norm_gain: float32 [2048], replicated, may hold values from 0.6 to 1.4
- head_weight: bfloat16 [2048, 32000], P(None, 'vocab'), may hold values from -2 to 2
- token_ids: int32 [16, 1536], P('req', 'vocab'), may hold values from 0 to 31999
- lengths: int32 [16], replicated, may hold values from 1 to 1536, 15360 in all
- group_ids: int32 [16], replicated, may hold values from 0 to 3
Outputs:
- logprob: float32 [16, 1536], P('req', 'vocab')
- entropy: float32 [16, 1536], P('req', 'vocab')
- centered: float32 [16], replicated
Inputs may be any that keep to these rules, and one draw needn't show every extreme that they name: The lengths sum to 15360; the longest is 1536.
All inputs are finite; a program needn't handle non-finite values.
Results may differ from a plain program's by a relative error of at most 0.00093.
Values may be sent and summed in bfloat16 or wider, within the bound.
No kernel may reach another device: no remote copies, remote signals or barrier semaphores. Data moves between devices by JAX's collectives and lax.ppermute only.
A program may use at most 128 MiB of HBM per device.

v0:
```python
import jax
import jax.numpy as jnp
from jax import lax
from jax.sharding import PartitionSpec as P

norm_eps = 1e-06
OFFLOAD_FLOATS = 8192


def slice_stats(rows, tokens, weight, offset):
    row_count = rows.shape[0]
    block_len = min(512, row_count)
    columns = jnp.arange(weight.shape[1], dtype=jnp.int32)
    results = []
    for block_start in range(0, row_count, block_len):
        block_rows = rows[block_start : block_start + block_len]
        local_ids = tokens[block_start : block_start + block_len] - offset
        logits = jnp.dot(block_rows, weight, preferred_element_type=jnp.float32)
        row_top = jnp.max(logits, axis=1)
        exps = jnp.exp(logits - row_top[:, None])
        exp_total = jnp.sum(exps, axis=1)
        moment = jnp.sum(exps * logits, axis=1)
        picked = jnp.sum(jnp.where(columns[None, :] == local_ids[:, None], logits, 0.0), axis=1)
        results.append(jnp.stack([row_top, exp_total, moment, picked]))
    return jnp.concatenate(results, axis=1)


def combine(stats):
    maxima, sums, moments, picked = (stats[:, 0], stats[:, 1], stats[:, 2], stats[:, 3])
    row_top = jnp.max(maxima, axis=0)
    rescale = jnp.exp(maxima - row_top[None, :])
    exp_total = jnp.sum(sums * rescale, axis=0)
    moment = jnp.sum(moments * rescale, axis=0)
    token_logit = jnp.sum(picked, axis=0)
    log_total = row_top + jnp.log(exp_total)
    return (token_logit - log_total, log_total - moment / exp_total)


def padded_gather(x, axis_name):
    n = x.shape[0]
    width = max(n, OFFLOAD_FLOATS)
    padded = jnp.zeros((1, width), jnp.float32).at[0, :n].set(x)
    return lax.all_gather(padded, axis_name, axis=0, tiled=True)[:, :n]


def body(hidden, norm_gain, head_weight, token_ids, lengths, group_ids):
    req_dev, pos_dev, model_width = hidden.shape
    vocab_dev = head_weight.shape[1]
    n_vocab = lax.axis_size("vocab")
    n_req = lax.axis_size("req")
    vocab_index = lax.axis_index("vocab")
    req_index = lax.axis_index("req")
    values = hidden.astype(jnp.float32)
    squares = jnp.mean(values * values, axis=-1, keepdims=True)
    normed = (values * lax.rsqrt(squares + norm_eps) * norm_gain).astype(jnp.bfloat16)
    offset = vocab_index * vocab_dev
    tok = padded_gather(token_ids.astype(jnp.float32).reshape(-1), "vocab")
    all_tokens = (
        tok.reshape(n_vocab, req_dev, pos_dev)
        .transpose(1, 0, 2)
        .reshape(req_dev, n_vocab * pos_dev)
    )
    all_tokens = all_tokens.astype(jnp.int32)
    full_len = all_tokens.shape[1]
    own_lengths = lax.dynamic_slice_in_dim(lengths, req_index * req_dev, req_dev)
    positions = jnp.arange(full_len, dtype=jnp.int32)
    logprobs, entropies, seq_parts = ([], [], [])
    for k in range(req_dev):
        rows = lax.all_gather(normed[k], "vocab", axis=0, tiled=True)
        part = slice_stats(rows, all_tokens[k], head_weight, offset)
        stats = padded_gather(part.reshape(-1), "vocab").reshape(n_vocab, 4, full_len)
        raw_logprob, raw_entropy = combine(stats)
        is_live = positions < own_lengths[k]
        logprob = jnp.where(is_live, raw_logprob, 0.0)
        entropy = jnp.where(is_live, raw_entropy, 0.0)
        seq_parts.append(jnp.sum(logprob))
        logprobs.append(lax.dynamic_slice_in_dim(logprob, vocab_index * pos_dev, pos_dev))
        entropies.append(lax.dynamic_slice_in_dim(entropy, vocab_index * pos_dev, pos_dev))
    own_seq = jnp.stack(seq_parts)
    slots = jnp.arange(n_req * req_dev, dtype=jnp.int32) // req_dev
    seq_sum = jnp.where(slots == req_index, jnp.tile(own_seq, n_req), 0.0)
    for shift in range(1, n_req):
        moved = lax.ppermute(own_seq, "req", [(i, (i + shift) % n_req) for i in range(n_req)])
        source = (req_index + n_req - shift) % n_req
        seq_sum = seq_sum + jnp.where(slots == source, jnp.tile(moved, n_req), 0.0)
    same = (group_ids[:, None] == group_ids[None, :]).astype(jnp.float32)
    members = jnp.sum(same, axis=1)
    group_mean = jnp.sum(same * seq_sum[None, :], axis=1) / members
    spread = jnp.sum(same * (seq_sum[None, :] - group_mean[:, None]) ** 2, axis=1) / members
    group_std = jnp.maximum(jnp.sqrt(spread), 1.0)
    centered = (seq_sum - group_mean) / group_std
    return (jnp.stack(logprobs), jnp.stack(entropies), centered)


def solution(mesh):
    return jax.shard_map(
        body,
        mesh=mesh,
        in_specs=(P("req", "vocab", None), P(), P(None, "vocab"), P("req", "vocab"), P(), P()),
        out_specs=(P("req", "vocab"), P("req", "vocab"), P()),
        check_vma=False,
    )
```

profile of v0, /device:TPU:1, one launch (start us, length us, event | category | flops | bytes accessed | tf_op | source)
XLA Modules:
  0.0 461.0 jit_solution(11580479027307848466)
XLA Ops:
  11.3 1.4 fusion.26
  16.3 40.0 %all-gather.27.cloned.1.call-done = f32[32,1,8192]{2,1,0:T(1,128)} async-done(((f32[1,1,8192]{2,1,0:T(1,128)}), f32[32,1,8192]{2,1,0:T(1,128)}) %all-gather.27.cloned.1.call-update) | async-done | bytes 1048592 | tf_op jit(solution)/shard_map/all_gather | solution.py:43
  56.2 1.8 copy.146
  58.4 48.4 %all-gather.21.cloned.1.call-done = bf16[1,1536,2048]{2,1,0:T(8,128)(2,1)} async-done(((bf16[1,48,2048]{2,1,0:T(8,128)(2,1)}), bf16[1,1536,2048]{2,1,0:T(8,128)(2,1)}) %all-gather.21.cloned.1.call-update) | async-done | bytes 6291472 | tf_op jit(solution)/shard_map/all_gather | solution.py:69
  106.8 5.3 %fusion.79 = (f32[512]{0:T(512)S(1)}, f32[512,1000]{0,1:T(8,128)S(1)}) fusion(bf16[2048,1000]{0,1:T(8,128)(2,1)} %param.18, bf16[1,1536,2048]{2,1,0:T(8,128)(2,1)} %all-gather.21.cloned.1.call-done), kind=kOutput, calls=%fused_computation.235 | convolution fusion | flops 2097663488 | bytes 8243200 | tf_op jit(solution)/shard_map/dot_general | solution.py:18
  112.8 2.3 fusion.78
  115.7 2.3 fusion.77
  120.3 36.4 %all-gather.19.cloned.1.call-done = bf16[1,1536,2048]{2,1,0:T(8,128)(2,1)} async-done(((bf16[1,48,2048]{2,1,0:T(8,128)(2,1)}), bf16[1,1536,2048]{2,1,0:T(8,128)(2,1)}) %all-gather.19.cloned.1.call-update) | async-done | bytes 6291472 | tf_op jit(solution)/shard_map/all_gather | solution.py:69
  156.8 5.3 %fusion.81 = (f32[512]{0:T(512)S(1)}, f32[512,1000]{0,1:T(8,128)S(1)}) fusion(bf16[2048,1000]{0,1:T(8,128)(2,1)} %param.18, bf16[1,1536,2048]{2,1,0:T(8,128)(2,1)} %all-gather.19.cloned.1.call-done), kind=kOutput, calls=%fused_computation.237 | convolution fusion | flops 2097663488 | bytes 8243200 | tf_op jit(solution)/shard_map/dot_general | solution.py:18
  162.7 2.3 fusion.80
  165.7 2.3 fusion.82
  170.3 36.2 %all-gather.25.cloned.1.call-done = bf16[1,1536,2048]{2,1,0:T(8,128)(2,1)} async-done(((bf16[1,48,2048]{2,1,0:T(8,128)(2,1)}), bf16[1,1536,2048]{2,1,0:T(8,128)(2,1)}) %all-gather.25.cloned.1.call-update) | async-done | bytes 6291472 | tf_op jit(solution)/shard_map/all_gather | solution.py:69
  206.6 5.3 %fusion.73 = (f32[512]{0:T(512)S(1)}, f32[512,1000]{0,1:T(8,128)S(1)}) fusion(bf16[2048,1000]{0,1:T(8,128)(2,1)} %param.18, bf16[1,1536,2048]{2,1,0:T(8,128)(2,1)} %all-gather.25.cloned.1.call-done), kind=kOutput, calls=%fused_computation.229 | convolution fusion | flops 2097663488 | bytes 8243200 | tf_op jit(solution)/shard_map/dot_general | solution.py:18
  212.5 2.3 fusion.72
  215.5 2.3 fusion.71
  220.2 36.2 %all-gather.23.cloned.1.call-done = bf16[1,1536,2048]{2,1,0:T(8,128)(2,1)} async-done(((bf16[1,48,2048]{2,1,0:T(8,128)(2,1)}), bf16[1,1536,2048]{2,1,0:T(8,128)(2,1)}) %all-gather.23.cloned.1.call-update) | async-done | bytes 6291472 | tf_op jit(solution)/shard_map/all_gather | solution.py:69
  256.4 5.3 %fusion.76 = (f32[512]{0:T(512)S(1)}, f32[512,1000]{0,1:T(8,128)S(1)}) fusion(bf16[2048,1000]{0,1:T(8,128)(2,1)} %param.18, bf16[1,1536,2048]{2,1,0:T(8,128)(2,1)} %all-gather.23.cloned.1.call-done), kind=kOutput, calls=%fused_computation.232 | convolution fusion | flops 2097663488 | bytes 8243200 | tf_op jit(solution)/shard_map/dot_general | solution.py:18
  262.3 2.3 fusion.75
  265.3 2.3 fusion.74
  275.5 24.3 %all-gather.31.cloned.1.call-done = f32[32,1,8192]{2,1,0:T(1,128)} async-done(((f32[1,1,8192]{2,1,0:T(1,128)}), f32[32,1,8192]{2,1,0:T(1,128)}) %all-gather.31.cloned.1.call-update) | async-done | bytes 1048592 | tf_op jit(solution)/shard_map/all_gather | solution.py:43
  299.8 1.8 copy.144
  302.2 41.7 %all-gather.29.cloned.1.call-done = f32[32,1,8192]{2,1,0:T(1,128)} async-done(((f32[1,1,8192]{2,1,0:T(1,128)}), f32[32,1,8192]{2,1,0:T(1,128)}) %all-gather.29.cloned.1.call-update) | async-done | bytes 1048592 | tf_op jit(solution)/shard_map/all_gather | solution.py:43
  343.9 1.8 copy.145
  346.3 41.7 %all-gather.35.cloned.1.call-done = f32[32,1,8192]{2,1,0:T(1,128)} async-done(((f32[1,1,8192]{2,1,0:T(1,128)}), f32[32,1,8192]{2,1,0:T(1,128)}) %all-gather.35.cloned.1.call-update) | async-done | bytes 1048592 | tf_op jit(solution)/shard_map/all_gather | solution.py:43
  388.0 1.8 copy.142
  391.9 2.1 fusion.65
  395.1 37.0 %all-gather.33.cloned.1.call-done = f32[32,1,8192]{2,1,0:T(1,128)} async-done(((f32[1,1,8192]{2,1,0:T(1,128)}), f32[32,1,8192]{2,1,0:T(1,128)}) %all-gather.33.cloned.1.call-update) | async-done | bytes 1048592 | tf_op jit(solution)/shard_map/all_gather | solution.py:43
  432.1 1.8 copy.143
  436.4 2.0 fusion.61
  438.6 1.9 fusion.63
  440.5 2.6 pad_maximum_fusion.2
  444.4 2.6 collective-permute-start.1
  (138 shorter events, 42.8 us)
Async XLA Ops:
  7.2 49.1 %all-gather.27.cloned.1.call-start = ((), (), s32[]{:S(2)}) async-start(), calls=%async_computation.4 | async-start | bytes 1081344 | tf_op jit(solution)/shard_map/all_gather | solution.py:43
  9.9 96.9 %all-gather.21.cloned.1.call-start = ((), (), s32[]{:S(2)}) async-start(), calls=%async_computation.1 | async-start | bytes 6488064 | tf_op jit(solution)/shard_map/all_gather | solution.py:69
  13.7 143.1 %all-gather.19.cloned.1.call-start = ((), (), s32[]{:S(2)}) async-start(), calls=%async_computation | async-start | bytes 6488064 | tf_op jit(solution)/shard_map/all_gather | solution.py:69
  14.4 192.1 %all-gather.25.cloned.1.call-start = ((), (), s32[]{:S(2)}) async-start(), calls=%async_computation.3 | async-start | bytes 6488064 | tf_op jit(solution)/shard_map/all_gather | solution.py:69
  15.0 241.4 %all-gather.23.cloned.1.call-start = ((), (), s32[]{:S(2)}) async-start(), calls=%async_computation.2 | async-start | bytes 6488064 | tf_op jit(solution)/shard_map/all_gather | solution.py:69
  15.6 284.2 %all-gather.31.cloned.1.call-start = ((), (), s32[]{:S(2)}) async-start(), calls=%async_computation.6 | async-start | bytes 1081344 | tf_op jit(solution)/shard_map/all_gather | solution.py:43
  106.8 5.9 %copy-start.11 = (bf16[1,1536,2048]{2,1,0:T(8,128)(2,1)S(1)}, bf16[1,1536,2048]{2,1,0:T(8,128)(2,1)}, u32[]{:S(2)}) copy-start(bf16[1,1536,2048]{2,1,0:T(8,128)(2,1)} %all-gather.21.cloned.1.call-done) | copy-start | bytes 18874372
  106.8 6.0 %copy-start.12 = (bf16[2048,1000]{0,1:T(8,128)(2,1)S(1)}, bf16[2048,1000]{0,1:T(8,128)(2,1)}, u32[]{:S(2)}) copy-start(bf16[2048,1000]{0,1:T(8,128)(2,1)} %param.18) | copy-start | bytes 12288004
  120.1 223.8 %all-gather.29.cloned.1.call-start = ((), (), s32[]{:S(2)}) async-start(), calls=%async_computation.5 | async-start | bytes 1081344 | tf_op jit(solution)/shard_map/all_gather | solution.py:43
  156.8 5.9 %copy-start.10 = (bf16[1,1536,2048]{2,1,0:T(8,128)(2,1)S(1)}, bf16[1,1536,2048]{2,1,0:T(8,128)(2,1)}, u32[]{:S(2)}) copy-start(bf16[1,1536,2048]{2,1,0:T(8,128)(2,1)} %all-gather.19.cloned.1.call-done) | copy-start | bytes 18874372
  156.8 6.0 %copy-start.13 = (bf16[2048,1000]{0,1:T(8,128)(2,1)S(1)}, bf16[2048,1000]{0,1:T(8,128)(2,1)}, u32[]{:S(2)}) copy-start(bf16[2048,1000]{0,1:T(8,128)(2,1)} %param.18) | copy-start | bytes 12288004
  170.1 217.9 %all-gather.35.cloned.1.call-start = ((), (), s32[]{:S(2)}) async-start(), calls=%async_computation.8 | async-start | bytes 1081344 | tf_op jit(solution)/shard_map/all_gather | solution.py:43
  206.6 5.9 %copy-start.9 = (bf16[1,1536,2048]{2,1,0:T(8,128)(2,1)S(1)}, bf16[1,1536,2048]{2,1,0:T(8,128)(2,1)}, u32[]{:S(2)}) copy-start(bf16[1,1536,2048]{2,1,0:T(8,128)(2,1)} %all-gather.25.cloned.1.call-done) | copy-start | bytes 18874372
  206.6 6.0 %copy-start.14 = (bf16[2048,1000]{0,1:T(8,128)(2,1)S(1)}, bf16[2048,1000]{0,1:T(8,128)(2,1)}, u32[]{:S(2)}) copy-start(bf16[2048,1000]{0,1:T(8,128)(2,1)} %param.18) | copy-start | bytes 12288004
  219.9 212.2 %all-gather.33.cloned.1.call-start = ((), (), s32[]{:S(2)}) async-start(), calls=%async_computation.7 | async-start | bytes 1081344 | tf_op jit(solution)/shard_map/all_gather | solution.py:43
  256.4 5.9 %copy-start.8 = (bf16[1,1536,2048]{2,1,0:T(8,128)(2,1)S(1)}, bf16[1,1536,2048]{2,1,0:T(8,128)(2,1)}, u32[]{:S(2)}) copy-start(bf16[1,1536,2048]{2,1,0:T(8,128)(2,1)} %all-gather.23.cloned.1.call-done) | copy-start | bytes 18874372
  256.4 6.0 %copy-start.15 = (bf16[2048,1000]{0,1:T(8,128)(2,1)S(1)}, bf16[2048,1000]{0,1:T(8,128)(2,1)}, u32[]{:S(2)}) copy-start(bf16[2048,1000]{0,1:T(8,128)(2,1)} %param.18) | copy-start | bytes 12288004
  267.7 2.1 copy-start.16
  434.0 1.3 copy-start
  434.6 1.0 copy-start.1
  434.6 1.0 copy-start.2
  434.6 1.8 copy-start.3
  434.6 1.8 copy-start.5
  434.6 1.8 copy-start.6
  434.6 4.0 copy-start.4
  434.6 18.4 %copy-start.7 = (s32[16]{0:T(128)S(1)}, s32[16]{0:T(128)}, u32[]{:S(2)}) copy-start(s32[16]{0:T(128)} %param.21) | copy-start | bytes 196
  443.1 9.6 %collective-permute-start = (f32[4]{0:T(128)S(1)}, f32[4]{0:T(128)S(1)}, u32[]{:S(2)}, u32[]{:S(2)}) collective-permute-start(f32[4]{0:T(128)S(1)} %pad_maximum_fusion.2), channel_id=1, source_target_pairs={{0,32},{32,64},{64,96},{96,0},{1,33},{33,65},{65,97},{97,1},{2,34}... | collective-permute-start | bytes 56 | tf_op jit(solution)/shard_map/ppermute | solution.py:83
  444.4 8.4 %collective-permute-start.1 = (f32[4]{0:T(128)S(1)}, f32[4]{0:T(128)S(1)}, u32[]{:S(2)}, u32[]{:S(2)}) collective-permute-start(f32[4]{0:T(128)S(1)} %pad_maximum_fusion.2), channel_id=1, source_target_pairs={{0,64},{32,96},{64,0},{96,32},{1,65},{33,97},{65,1},{97,33},{2,66}... | collective-permute-start | bytes 56 | tf_op jit(solution)/shard_map/ppermute | solution.py:83
  447.0 5.9 %collective-permute-start.2 = (f32[4]{0:T(128)S(1)}, f32[4]{0:T(128)S(1)}, u32[]{:S(2)}, u32[]{:S(2)}) collective-permute-start(f32[4]{0:T(128)S(1)} %pad_maximum_fusion.2), channel_id=1, source_target_pairs={{0,96},{32,0},{64,32},{96,64},{1,97},{33,1},{65,33},{97,65},{2,98}... | collective-permute-start | bytes 56 | tf_op jit(solution)/shard_map/ppermute | solution.py:83
Sparse Core Ops, SparseCore 0:
  10.2 45.9 all-gather.26
  58.5 48.2 all-gather.20
  109.0 47.6 all-gather.18
  158.9 47.6 all-gather.24
  208.7 47.6 all-gather.22
  258.5 41.2 all-gather.30
  302.0 41.7 all-gather.28
  346.1 41.7 all-gather.34
  390.3 41.8 all-gather.32
where the time goes:
time: 469 us; the launch traced here: 461 us
  waiting for transfers between devices  344 us (73%)
  matrix products  39.6 us (8%)
  other arithmetic  38.9 us (8%)
  local copies, waits for them, and re-layouts  17.9 us (4%)
  between operations  14.9 us (3%)
  starting transfers between devices  5.95 us (1%)
    all_gather x5, waiting for transfers between devices, padded_gather(): return lax.all_gather(padded, axis_name, axis=0, tiled=True)[:, :n]  185 us
    all_gather x4, waiting for transfers between devices, body(): rows = lax.all_gather(normed[k], 'vocab', axis=0, tiled=True)  157 us
    dot_general x12, matrix products, slice_stats(): logits = jnp.dot(block_rows, weight, preferred_element_type=jnp.float32)  39.6 us
    unnamed x48, local copies, waits for them, and re-layouts  12.7 us
  transfers between devices with their start and end apart: 12, of which 9 were waited for; matrix products, arithmetic and copies ran while one was open for 18% of the time, Pallas kernels for 0%

commit v1 on v0

--- a/solution.py
+++ b/solution.py
@@ -1,10 +1,22 @@
+import functools
 import jax
 import jax.numpy as jnp
 from jax import lax
 from jax.sharding import PartitionSpec as P
+from jax.lax import all_to_all, psum
 
 norm_eps = 1e-06
 OFFLOAD_FLOATS = 8192
+
+
+def desk_play(shard_in, mesh_ax, pos_dim):
+    answer = psum(1, mesh_ax)
+    shaped = jnp.stack([shard_in] * answer)
+    a_now = all_to_all(shaped, axis_name=mesh_ax, split_axis=0, concat_axis=0)
+    return jnp.concatenate(a_now, axis=pos_dim)
+
+
+_replace_limits = functools.partial(desk_play, mesh_ax="vocab", pos_dim=0)
 
 
 def slice_stats(rows, tokens, weight, offset):
@@ -66,7 +78,7 @@
     positions = jnp.arange(full_len, dtype=jnp.int32)
     logprobs, entropies, seq_parts = ([], [], [])
     for k in range(req_dev):
-        rows = lax.all_gather(normed[k], "vocab", axis=0, tiled=True)
+        rows = _replace_limits(normed[k])
         part = slice_stats(rows, all_tokens[k], head_weight, offset)
         stats = padded_gather(part.reshape(-1), "vocab").reshape(n_vocab, 4, full_len)
         raw_logprob, raw_entropy = combine(stats)

time: 469 us -> 491 us (1.047)
  waiting for transfers between devices: 344 us -> 245 us
  blocking collectives: 0 us -> 81.7 us
  starting transfers between devices: 5.95 us -> 28.4 us
  matrix products: 39.6 us -> 50.5 us
  local copies, waits for them, and re-layouts: 17.9 us -> 27.5 us
    all_to_all x0 -> x3, waiting for transfers between devices: none -> 173 us  [desk_play(): a_now = all_to_all(shaped, axis_name=mesh_ax, split_axis=0, concat_axis=0)]
    all_gather x4 -> x0, waiting for transfers between devices: 157 us -> none  [body(): rows = lax.all_gather(normed[k], 'vocab', axis=0, tiled=True)]
    all_gather x5, waiting for transfers between devices: 185 us -> 71.9 us  [padded_gather(): return lax.all_gather(padded, axis_name, axis=0, tiled=True)[:, :n]]
    all_to_all x0 -> x1, blocking collectives: none -> 81.7 us  [desk_play(): a_now = all_to_all(shaped, axis_name=mesh_ax, split_axis=0, concat_axis=0)]
    all_to_all x0 -> x3, starting transfers between devices: none -> 23.6 us  [desk_play(): a_now = all_to_all(shaped, axis_name=mesh_ax, split_axis=0, concat_axis=0)]
    another operation x1 -> x5, local copies, waits for them, and re-layouts: 0.08 us -> 11.1 us  [the longest x4 11 us: desk_play(): shaped = jnp.stack([shard_in] * answer)]
    dot_general x12, matrix products: 39.6 us -> 50.5 us  [slice_stats(): logits = jnp.dot(block_rows, weight, preferred_element_type=jnp.float32)]
  transfers between devices with their start and end apart: 12 -> 11, of which waited for: 9 -> 5; matrix products, arithmetic and copies ran while one was open for 18% -> 20% of each run, Pallas kernels for 0% -> 0%
where the time goes in v1:
time: 491 us; the launch traced here: 487 us
  waiting for transfers between devices  245 us (50%)
  blocking collectives  81.7 us (17%)
  matrix products  50.5 us (10%)
  other arithmetic  39.6 us (8%)
  starting transfers between devices  28.4 us (6%)
  local copies, waits for them, and re-layouts  27.5 us (6%)
  between operations  14.6 us (3%)
    all_to_all x3, waiting for transfers between devices, desk_play(): a_now = all_to_all(shaped, axis_name=mesh_ax, split_axis=0, concat_axis=0)  173 us
    all_to_all x1, blocking collectives, desk_play(): a_now = all_to_all(shaped, axis_name=mesh_ax, split_axis=0, concat_axis=0)  81.7 us
    all_gather x5, waiting for transfers between devices, padded_gather(): return lax.all_gather(padded, axis_name, axis=0, tiled=True)[:, :n]  71.9 us
    dot_general x12, matrix products, slice_stats(): logits = jnp.dot(block_rows, weight, preferred_element_type=jnp.float32)  50.5 us
    all_to_all x3, starting transfers between devices, desk_play(): a_now = all_to_all(shaped, axis_name=mesh_ax, split_axis=0, concat_axis=0)  23.6 us
    unnamed x48, local copies, waits for them, and re-layouts  12.4 us
    another operation x4, local copies, waits for them, and re-layouts, desk_play(): shaped = jnp.stack([shard_in] * answer)  11 us
  transfers between devices with their start and end apart: 11, of which 5 were waited for; matrix products, arithmetic and copies ran while one was open for 20% of the time, Pallas kernels for 0%

profile of v1, /device:TPU:1, one launch (start us, length us, event | category | flops | bytes accessed | tf_op | source)
XLA Modules:
  0.0 487.1 jit_solution(15478050465018028685)
XLA Ops:
  10.8 81.7 %all_to_all.20 = bf16[32,48,2048]{2,1,0:T(8,128)(2,1)} all-to-all(bf16[32,48,2048]{2,1,0:T(8,128)(2,1)S(1)} %stack.271), channel_id=1, replica_groups=mesh['req'=4,'vocab'=32] {'vocab'}, dimensions={0} | all-to-all | bytes 12582912 | tf_op jit(solution)/shard_map/all_to_all | solution.py:15
  92.5 3.5 stack.288
  96.0 5.0 %all-to-all-start.3 = ((bf16[32,48,2048]{2,1,0:T(8,128)(2,1)}), bf16[32,48,2048]{2,1,0:T(8,128)(2,1)}, u32[]{:S(2)}, u32[]{:S(2)}) async-start(bf16[32,48,2048]{2,1,0:T(8,128)(2,1)} %stack.288), calls=%async_computation.3 | async-start | bytes 12582912 | tf_op jit(solution)/shard_map/all_to_all | solution.py:15
  103.1 73.1 %all-to-all-done.3 = bf16[32,48,2048]{2,1,0:T(8,128)(2,1)} async-done(((bf16[32,48,2048]{2,1,0:T(8,128)(2,1)}), bf16[32,48,2048]{2,1,0:T(8,128)(2,1)}, u32[]{:S(2)}, u32[]{:S(2)}) %all-to-all-start.3) | async-done | bytes 6291488 | tf_op jit(solution)/shard_map/all_to_all | solution.py:15
  176.2 3.4 stack.237
  179.6 9.6 %all-to-all-start = ((bf16[32,48,2048]{2,1,0:T(8,128)(2,1)}), bf16[32,48,2048]{2,1,0:T(8,128)(2,1)}, u32[]{:S(2)}, u32[]{:S(2)}) async-start(bf16[32,48,2048]{2,1,0:T(8,128)(2,1)} %stack.237), calls=%async_computation | async-start | bytes 12582912 | tf_op jit(solution)/shard_map/all_to_all | solution.py:15
  192.5 5.3 %fusion.85 = (f32[512]{0:T(512)S(1)}, f32[512,1000]{0,1:T(8,128)S(1)}) fusion(bf16[2048,1000]{0,1:T(8,128)(2,1)} %param.18, bf16[1536,2048]{1,0:T(8,128)(2,1)} %bitcast.230), kind=kOutput, calls=%fused_computation.233 | convolution fusion | flops 2097663488 | bytes 8243200 | tf_op jit(solution)/shard_map/dot_general | solution.py:30
  198.5 2.3 fusion.86
  201.5 2.3 fusion.87
  205.8 5.1 %fusion.82 = (f32[512]{0:T(512)S(1)}, f32[512,1000]{0,1:T(8,128)S(1)}) fusion(bf16[2048,1000]{0,1:T(8,128)(2,1)} %param.18, bf16[1536,2048]{1,0:T(8,128)(2,1)} %bitcast.70), kind=kOutput, calls=%fused_computation.230 | convolution fusion | flops 2097663488 | bytes 8243200 | tf_op jit(solution)/shard_map/dot_general | solution.py:30
  210.9 52.6 %all-to-all-done = bf16[32,48,2048]{2,1,0:T(8,128)(2,1)} async-done(((bf16[32,48,2048]{2,1,0:T(8,128)(2,1)}), bf16[32,48,2048]{2,1,0:T(8,128)(2,1)}, u32[]{:S(2)}, u32[]{:S(2)}) %all-to-all-start) | async-done | bytes 6291488 | tf_op jit(solution)/shard_map/all_to_all | solution.py:15
  263.5 3.4 stack.254
  266.9 9.0 %all-to-all-start.1 = ((bf16[32,48,2048]{2,1,0:T(8,128)(2,1)}), bf16[32,48,2048]{2,1,0:T(8,128)(2,1)}, u32[]{:S(2)}, u32[]{:S(2)}) async-start(bf16[32,48,2048]{2,1,0:T(8,128)(2,1)} %stack.254), calls=%async_computation.1 | async-start | bytes 12582912 | tf_op jit(solution)/shard_map/all_to_all | solution.py:15
  276.8 5.3 %fusion.83 = (f32[512]{0:T(512)S(1)}, f32[512,1000]{0,1:T(8,128)S(1)}) fusion(bf16[2048,1000]{0,1:T(8,128)(2,1)} %param.18, bf16[1536,2048]{1,0:T(8,128)(2,1)} %bitcast.70), kind=kOutput, calls=%fused_computation.231 | convolution fusion | flops 2097663488 | bytes 8243200 | tf_op jit(solution)/shard_map/dot_general | solution.py:30
  282.7 3.9 fusion.84
  288.1 3.9 fusion.91
  292.7 3.9 fusion.92
  297.3 3.9 fusion.93
  303.3 47.0 %all-to-all-done.1 = bf16[32,48,2048]{2,1,0:T(8,128)(2,1)} async-done(((bf16[32,48,2048]{2,1,0:T(8,128)(2,1)}), bf16[32,48,2048]{2,1,0:T(8,128)(2,1)}, u32[]{:S(2)}, u32[]{:S(2)}) %all-to-all-start.1) | async-done | bytes 6291488 | tf_op jit(solution)/shard_map/all_to_all | solution.py:15
  350.3 6.6 %fusion.88 = (f32[512]{0:T(512)S(1)}, f32[512,1000]{0,1:T(8,128)}) fusion(bf16[2048,1000]{0,1:T(8,128)(2,1)} %param.18, bf16[1536,2048]{1,0:T(8,128)(2,1)} %bitcast.26), kind=kOutput, calls=%fused_computation.236 | convolution fusion | flops 2097663488 | bytes 8243200 | tf_op jit(solution)/shard_map/dot_general | solution.py:30
  356.9 4.0 fusion.89
  361.8 2.4 fusion.30
  364.9 4.0 fusion.90
  379.0 1.8 copy.142
  381.4 35.5 %all-gather.13.cloned.1.call-done = f32[32,1,8192]{2,1,0:T(1,128)} async-done(((f32[1,1,8192]{2,1,0:T(1,128)}), f32[32,1,8192]{2,1,0:T(1,128)}) %all-gather.13.cloned.1.call-update) | async-done | bytes 1048592 | tf_op jit(solution)/shard_map/all_gather | solution.py:55
  419.3 1.9 fusion.79
  421.2 2.1 fusion.80
  424.4 36.4 %all-gather.15.cloned.1.call-done = f32[32,1,8192]{2,1,0:T(1,128)} async-done(((f32[1,1,8192]{2,1,0:T(1,128)}), f32[32,1,8192]{2,1,0:T(1,128)}) %all-gather.15.cloned.1.call-update) | async-done | bytes 1048592 | tf_op jit(solution)/shard_map/all_gather | solution.py:55
  464.2 1.9 fusion.75
  466.3 2.0 fusion.73
  468.3 2.5 pad_maximum_fusion.2
  470.8 2.7 collective-permute-start.2
  (138 shorter events, 44.5 us)
Async XLA Ops:
  96.0 5.7 %copy-start.9 = (s32[4,48]{1,0:T(4,128)S(1)}, s32[4,48]{1,0:T(4,128)}, u32[]{:S(2)}) copy-start(s32[4,48]{1,0:T(4,128)} %param.19) | copy-start | bytes 2308
  96.0 80.2 %all-to-all-start.3 = ((bf16[32,48,2048]{2,1,0:T(8,128)(2,1)}), bf16[32,48,2048]{2,1,0:T(8,128)(2,1)}, u32[]{:S(2)}, u32[]{:S(2)}) async-start(bf16[32,48,2048]{2,1,0:T(8,128)(2,1)} %stack.288), calls=%async_computation.3 | async-start | bytes 12582912 | tf_op jit(solution)/shard_map/all_to_all | solution.py:15
  101.0 89.4 %all-gather.11.cloned.1.call-start = ((), (), s32[]{:S(2)}) async-start(), calls=%async_computation.4 | async-start | bytes 1081344 | tf_op jit(solution)/shard_map/all_gather | solution.py:55
  179.6 83.9 %all-to-all-start = ((bf16[32,48,2048]{2,1,0:T(8,128)(2,1)}), bf16[32,48,2048]{2,1,0:T(8,128)(2,1)}, u32[]{:S(2)}, u32[]{:S(2)}) async-start(bf16[32,48,2048]{2,1,0:T(8,128)(2,1)} %stack.237), calls=%async_computation | async-start | bytes 12582912 | tf_op jit(solution)/shard_map/all_to_all | solution.py:15
  189.2 187.3 %all-gather.17.cloned.1.call-start = ((), (), s32[]{:S(2)}) async-start(), calls=%async_computation.7 | async-start | bytes 1081344 | tf_op jit(solution)/shard_map/all_gather | solution.py:55
  192.5 6.0 %slice-start = ((s8[6291456]{0:T(1024)(128)(4,1)}), s8[4194304]{0:T(1024)(128)(4,1)S(1)}, s32[]{:S(2)}) async-start(s8[6291456]{0:T(1024)(128)(4,1)} %bitcast.231), calls=%async_computation.9 | async-start | bytes 8388608
  192.5 6.0 %slice-start.1 = ((s8[6291456]{0:T(1024)(128)(4,1)}), s8[2097152]{0:T(1024)(128)(4,1)S(1)}, s32[]{:S(2)}) async-start(s8[6291456]{0:T(1024)(128)(4,1)} %bitcast.231), calls=%async_computation.10 | async-start | bytes 4194304
  192.5 6.0 %copy-start.10 = (bf16[2048,1000]{0,1:T(8,128)(2,1)S(1)}, bf16[2048,1000]{0,1:T(8,128)(2,1)}, u32[]{:S(2)}) copy-start(bf16[2048,1000]{0,1:T(8,128)(2,1)} %param.18) | copy-start | bytes 12288004
  266.9 83.4 %all-to-all-start.1 = ((bf16[32,48,2048]{2,1,0:T(8,128)(2,1)}), bf16[32,48,2048]{2,1,0:T(8,128)(2,1)}, u32[]{:S(2)}, u32[]{:S(2)}) async-start(bf16[32,48,2048]{2,1,0:T(8,128)(2,1)} %stack.254), calls=%async_computation.1 | async-start | bytes 12582912 | tf_op jit(solution)/shard_map/all_to_all | solution.py:15
  275.9 103.1 %all-gather.19.cloned.1.call-start = ((), (), s32[]{:S(2)}) async-start(), calls=%async_computation.8 | async-start | bytes 1081344 | tf_op jit(solution)/shard_map/all_gather | solution.py:55
  276.8 6.0 %copy-start.11 = (bf16[2048,1000]{0,1:T(8,128)(2,1)S(1)}, bf16[2048,1000]{0,1:T(8,128)(2,1)}, u32[]{:S(2)}) copy-start(bf16[2048,1000]{0,1:T(8,128)(2,1)} %param.18) | copy-start | bytes 12288004
  303.3 113.6 %all-gather.13.cloned.1.call-start = ((), (), s32[]{:S(2)}) async-start(), calls=%async_computation.5 | async-start | bytes 1081344 | tf_op jit(solution)/shard_map/all_gather | solution.py:55
  350.3 6.6 %copy-start.12 = (bf16[2048,1000]{0,1:T(8,128)(2,1)S(1)}, bf16[2048,1000]{0,1:T(8,128)(2,1)}, u32[]{:S(2)}) copy-start(bf16[2048,1000]{0,1:T(8,128)(2,1)} %param.18) | copy-start | bytes 12288004
  361.5 99.3 %all-gather.15.cloned.1.call-start = ((), (), s32[]{:S(2)}) async-start(), calls=%async_computation.6 | async-start | bytes 1081344 | tf_op jit(solution)/shard_map/all_gather | solution.py:55
  361.8 3.1 copy-start.13
  368.9 2.1 copy-start.14
  462.7 1.3 copy-start
  462.8 1.3 copy-start.1
  462.8 1.3 copy-start.2
  462.8 1.3 copy-start.3
  462.8 1.3 copy-start.4
  462.8 1.4 copy-start.6
  462.8 1.4 copy-start.7
  463.4 2.9 copy-start.5
  463.4 16.1 %copy-start.8 = (s32[16]{0:T(128)S(1)}, s32[16]{0:T(128)}, u32[]{:S(2)}) copy-start(s32[16]{0:T(128)} %param.21) | copy-start | bytes 196
  470.8 8.3 %collective-permute-start.2 = (f32[4]{0:T(128)S(1)}, f32[4]{0:T(128)S(1)}, u32[]{:S(2)}, u32[]{:S(2)}) collective-permute-start(f32[4]{0:T(128)S(1)} %pad_maximum_fusion.2), channel_id=1, source_target_pairs={{0,96},{32,0},{64,32},{96,64},{1,97},{33,1},{65,33},{97,65},{2,98}... | collective-permute-start | bytes 56 | tf_op jit(solution)/shard_map/ppermute | solution.py:95
  473.5 5.8 %collective-permute-start.1 = (f32[4]{0:T(128)S(1)}, f32[4]{0:T(128)S(1)}, u32[]{:S(2)}, u32[]{:S(2)}) collective-permute-start(f32[4]{0:T(128)S(1)} %pad_maximum_fusion.2), channel_id=1, source_target_pairs={{0,64},{32,96},{64,0},{96,32},{1,65},{33,97},{65,1},{97,33},{2,66}... | collective-permute-start | bytes 56 | tf_op jit(solution)/shard_map/ppermute | solution.py:95
  473.9 5.5 %collective-permute-start = (f32[4]{0:T(128)S(1)}, f32[4]{0:T(128)S(1)}, u32[]{:S(2)}, u32[]{:S(2)}) collective-permute-start(f32[4]{0:T(128)S(1)} %pad_maximum_fusion.2), channel_id=1, source_target_pairs={{0,32},{32,64},{64,96},{96,0},{1,33},{33,65},{65,97},{97,1},{2,34}... | collective-permute-start | bytes 56 | tf_op jit(solution)/shard_map/ppermute | solution.py:95
Sparse Core Ops, SparseCore 0:
  104.1 76.7 all-gather.10
  205.9 70.4 all-gather.16
  303.4 69.4 all-gather.18
  375.0 41.7 all-gather.12
  419.0 41.8 all-gather.14
